TPU v7x, 32 devices: a whole 2x2x4 slice. The times are simulated.
32 devices in a mesh: tm: 8 (over y, x, core), space: 4 (over z).
Axes of the slice: x: 2, y: 2, z: 4, core: 2. Of those that a mesh axis runs over, the one named last changes fastest.
Arguments:
- queries: bfloat16 [8, 4, 128, 1024], P('tm', 'space'), may hold values from -30 to 30
- key_vectors: bfloat16 [8, 4, 128, 1024], P('tm', 'space'), may hold values from -30 to 30
- value_vectors: bfloat16 [8, 4, 128, 1024], P('tm', 'space'), may hold values from -6 to 6
- key_blocks: int32 [8, 4, 2, 32], P('tm', 'space'), may hold values from 0 to 63, as said below
- block_count: int32 [8, 4, 2], P('tm', 'space'), may hold values from 1 to 32, as said below
Outputs:
- attention_out: bfloat16 [8, 4, 128, 1024], P('tm', 'space')
Inputs may be any that keep to these rules, and one draw needn't show every extreme that they name: `key_blocks`: A row's entries are distinct ids of blocks in the query block's own band or an adjacent one, of any frame group; its first entry is the query block itself. Only the first block_count entries of a list are used; on some devices a list uses all 32.
All inputs are finite; a program needn't handle non-finite values.
Results may differ from a plain program's by a relative error of at most 0.0044.
Values may be sent and summed in bfloat16 or wider, within the bound.
No kernel may reach another device: no remote copies, remote signals or barrier semaphores. Data moves between devices by JAX's collectives and lax.ppermute only.
A program may use at most 128 MiB of HBM per device.

v0:
```python
import functools

import jax
import jax.numpy as jnp
from jax import lax
from jax.experimental import pallas as pl
from jax.experimental.pallas import tpu as pltpu
from jax.sharding import PartitionSpec as P

HEADS = 8
HDIM = 128
BLOCK = 64
PICKS = 32


def with_halo(cells, sides, width):
    for axis, dim in sides:
        count = lax.axis_size(axis)
        ends = count - 1
        head = lax.slice_in_dim(cells, 0, width, axis=dim)
        tail = lax.slice_in_dim(cells, cells.shape[dim] - width, cells.shape[dim], axis=dim)
        cells = jnp.concatenate(
            [
                lax.ppermute(tail, axis, [(i, (i + 1) % count) for i in range(ends)]),
                cells,
                lax.ppermute(head, axis, [((i + 1) % count, i) for i in range(ends)]),
            ],
            axis=dim,
        )
    return cells


def attend_kernel(where_ref, counts_ref, q_ref, *rest, blocks_here, pieces):
    sources = rest[:pieces]
    o_ref, kbuf, vbuf, sems = rest[pieces:]
    feature_width = q_ref.shape[1]
    bands_held = sources[0].shape[0] // 2

    def copies(qb, p, source):
        at = 2 * (qb * PICKS + p)
        row = where_ref[at + 1]
        rows = pl.ds(pl.multiple_of(p * BLOCK, BLOCK), BLOCK)
        k_copy = pltpu.make_async_copy(source.at[row], kbuf.at[qb, rows], sems.at[0, qb, p])
        v_copy = pltpu.make_async_copy(source.at[bands_held + row], vbuf.at[qb, rows], sems.at[1, qb, p])
        return k_copy, v_copy

    for qb in range(blocks_here):
        count = counts_ref[qb]

        def start(p, carry, qb=qb):
            piece = where_ref[2 * (qb * PICKS + p)]
            for j in range(pieces):
                @pl.when(piece == j)
                def _(j=j):
                    for c in copies(qb, p, sources[j]):
                        c.start()
            return carry

        def clear(p, carry, qb=qb):
            rows = pl.ds(pl.multiple_of(p * BLOCK, BLOCK), BLOCK)
            vbuf[qb, rows, :] = jnp.zeros((BLOCK, feature_width), vbuf.dtype)
            return carry

        lax.fori_loop(0, count, start, 0)
        lax.fori_loop(count, PICKS, clear, 0)

    for qb in range(blocks_here):
        count = counts_ref[qb]

        def finish(p, carry, qb=qb):
            for c in copies(qb, p, sources[0]):
                c.wait()
            return carry

        lax.fori_loop(0, count, finish, 0)
        column = lax.broadcasted_iota(jnp.int32, (BLOCK, PICKS * BLOCK), 1)
        usable = column < count * BLOCK
        for h in range(HEADS):
            cols = slice(h * HDIM, (h + 1) * HDIM)
            q_h = q_ref[qb * BLOCK:(qb + 1) * BLOCK, cols]
            k_h = kbuf[qb, :, cols]
            v_h = vbuf[qb, :, cols]
            scores = lax.dot_general(
                q_h, k_h, (((1,), (1,)), ((), ())), preferred_element_type=jnp.float32
            ) * HDIM ** (-0.5)
            scores = jnp.where(usable, scores, -1e30)
            peaks = jnp.max(scores, axis=-1, keepdims=True)
            weights = jnp.exp(scores - peaks)
            totals = jnp.sum(weights, axis=-1, keepdims=True)
            rounded = weights.astype(jnp.bfloat16)
            blended = jnp.dot(rounded, v_h, preferred_element_type=jnp.float32)
            o_ref[qb * BLOCK:(qb + 1) * BLOCK, cols] = (blended / totals).astype(o_ref.dtype)


def attend(query_rows, sources, where, counts):
    tokens_here, feature_width = query_rows.shape
    blocks_here = tokens_here // BLOCK
    kernel = functools.partial(attend_kernel, blocks_here=blocks_here, pieces=len(sources))
    grid_spec = pltpu.PrefetchScalarGridSpec(
        num_scalar_prefetch=2,
        grid=(1,),
        in_specs=[pl.BlockSpec((tokens_here, feature_width), lambda i, w, c: (0, 0))]
        + [pl.BlockSpec(memory_space=pl.ANY) for _ in sources],
        out_specs=pl.BlockSpec((tokens_here, feature_width), lambda i, w, c: (0, 0)),
        scratch_shapes=[
            pltpu.VMEM((blocks_here, PICKS * BLOCK, feature_width), query_rows.dtype),
            pltpu.VMEM((blocks_here, PICKS * BLOCK, feature_width), query_rows.dtype),
            pltpu.SemaphoreType.DMA((2, blocks_here, PICKS)),
        ],
    )
    return pl.pallas_call(
        kernel,
        grid_spec=grid_spec,
        out_shape=jax.ShapeDtypeStruct((tokens_here, feature_width), query_rows.dtype),
        compiler_params=pltpu.CompilerParams(vmem_limit_bytes=48 * 1024 * 1024),
    )(where, counts, query_rows, *sources)


def swap(piece, mask):
    count = lax.axis_size("tm")
    return lax.ppermute(piece, "tm", [(i, i ^ mask) for i in range(count)])


def on_device(queries, key_vectors, value_vectors, key_blocks, block_count):
    groups_here = queries.shape[0]
    tokens_here = queries.shape[2]
    feature_width = queries.shape[3]
    blocks_here = tokens_here // BLOCK
    members = lax.axis_size("tm")
    assert members & (members - 1) == 0 and members % 2 == 0
    stacked = jnp.stack([key_vectors, value_vectors])
    banded = with_halo(stacked, (("space", 2),), 1)
    tiles_per_piece = 2 * groups_here * 3 * blocks_here
    own = banded.reshape(tiles_per_piece, BLOCK, feature_width)
    pieces = [own] * members
    for mask in range(2, members, 2):
        pieces[mask] = swap(own, mask)
    for mask in range(0, members, 2):
        pieces[mask + 1] = swap(pieces[mask], 1)
    band_count = lax.axis_size("space")
    own_band = lax.axis_index("space")
    me = lax.axis_index("tm")
    listed = key_blocks.reshape(blocks_here, PICKS)
    within = listed % blocks_here
    band_of = listed // blocks_here % band_count
    group_of = listed // (blocks_here * band_count)
    holder = jnp.clip(group_of // groups_here, 0, members - 1)
    piece = jnp.bitwise_xor(holder, me)
    row = ((group_of % groups_here) * 3 + band_of - own_band + 1) * blocks_here + within
    row = jnp.clip(row, 0, tiles_per_piece // 2 - 1)
    where = jnp.stack([piece, row], axis=-1).reshape(-1).astype(jnp.int32)
    counts = jnp.clip(block_count.reshape(blocks_here), 1, PICKS).astype(jnp.int32)
    result = attend(queries.reshape(tokens_here, feature_width), pieces, where, counts)
    return result.reshape(queries.shape)


def solution(mesh):
    in_specs = (
        P("tm", "space", None, None),
        P("tm", "space", None, None),
        P("tm", "space", None, None),
        P("tm", "space", None, None),
        P("tm", "space", None),
    )
    out_specs = P("tm", "space", None, None)
    return jax.shard_map(
        on_device, mesh=mesh, in_specs=in_specs, out_specs=out_specs, check_vma=False
    )
```

profile of v0, /device:TPU:20, one launch (start us, length us, event | category | flops | bytes accessed | tf_op | source)
XLA Modules:
  0.0 114.5 jit_solution(16859291378824456271)
XLA Ops:
  0.0 1.1 pad_maximum_fusion.1
  1.1 0.0 copy-start.1
  1.1 0.0 copy-start.2
  1.1 0.0 copy-start
  1.1 2.5 %collective-permute-start.1 = (bf16[2,1,1,128,1024]{4,3,2,1,0:T(8,128)(2,1)S(1)}, bf16[2,1,1,128,1024]{4,3,2,1,0:T(8,128)(2,1)S(1)}, u32[]{:S(2)}, u32[]{:S(2)}) collective-permute-start(bf16[2,1,1,128,1024]{4,3,2,1,0:T(8,128)(2,1)S(1)} %pad_maximum_fusion.1), channel_id=1, source_target_pairs={{1,0},{2,1},{3,2},{5,4},{6,5},{7,6},{9,8},{10,9},{11,10},{13,12},{... | collective-permute-start | bytes 1572872 | tf_op jit(solution)/shard_map/ppermute | solution.py:26
  3.6 3.5 %collective-permute-start = (bf16[2,1,1,128,1024]{4,3,2,1,0:T(8,128)(2,1)S(1)}, bf16[2,1,1,128,1024]{4,3,2,1,0:T(8,128)(2,1)S(1)}, u32[]{:S(2)}, u32[]{:S(2)}) collective-permute-start(bf16[2,1,1,128,1024]{4,3,2,1,0:T(8,128)(2,1)S(1)} %pad_maximum_fusion.1), channel_id=1, source_target_pairs={{0,1},{1,2},{2,3},{4,5},{5,6},{6,7},{8,9},{9,10},{10,11},{12,13},{... | collective-permute-start | bytes 1572872 | tf_op jit(solution)/shard_map/ppermute | solution.py:24
  7.1 9.7 %collective-permute-done.1 = bf16[2,1,1,128,1024]{4,3,2,1,0:T(8,128)(2,1)S(1)} collective-permute-done((bf16[2,1,1,128,1024]{4,3,2,1,0:T(8,128)(2,1)S(1)}, bf16[2,1,1,128,1024]{4,3,2,1,0:T(8,128)(2,1)S(1)}, u32[]{:S(2)}, u32[]{:S(2)}) %collective-permute-start.1) | collective-permute-done | bytes 524320 | tf_op jit(solution)/shard_map/ppermute | solution.py:26
  16.8 2.1 %collective-permute-done = bf16[2,1,1,128,1024]{4,3,2,1,0:T(8,128)(2,1)S(1)} collective-permute-done((bf16[2,1,1,128,1024]{4,3,2,1,0:T(8,128)(2,1)S(1)}, bf16[2,1,1,128,1024]{4,3,2,1,0:T(8,128)(2,1)S(1)}, u32[]{:S(2)}, u32[]{:S(2)}) %collective-permute-start) | collective-permute-done | bytes 524320 | tf_op jit(solution)/shard_map/ppermute | solution.py:24
  18.9 1.2 %pad_maximum_fusion = bf16[2,1,3,128,1024]{4,3,2,1,0:T(8,128)(2,1)S(1)} fusion(bf16[2,1,1,128,1024]{4,3,2,1,0:T(8,128)(2,1)S(1)} %collective-permute-done.1, bf16[1,1,1,128,1024]{4,3,2,1,0:T(8,128)(2,1)} %bitcast.32, bf16[1,1,1,128,1024]{4,3,2,1,0:T(8,128)(2,1)} %bitcast.34, bf16[2,1,1,128,1024]{4,3,2,1,0:T(8,128)(2,1)S(1)} %collective-permute-done), kind=kLoop, calls=%fused_computation | loop fusion | flops 2359296 | bytes 3145728 | tf_op jit(solution)/shard_map/concatenate | solution.py:22
  20.1 1.5 %collective-permute-start.7 = (bf16[12,64,1024]{2,1,0:T(8,128)(2,1)S(1)}, bf16[12,64,1024]{2,1,0:T(8,128)(2,1)}, u32[]{:S(2)}, u32[]{:S(2)}) collective-permute-start(bf16[12,64,1024]{2,1,0:T(8,128)(2,1)S(1)} %bitcast.25), channel_id=1, source_target_pairs={{0,24},{4,28},{8,16},{12,20},{16,8},{20,12},{24,0},{28,4},{1,25},{... | collective-permute-start | bytes 4718600 | tf_op jit(solution)/shard_map/ppermute | solution.py:121
  21.6 1.5 %collective-permute-start.5 = (bf16[12,64,1024]{2,1,0:T(8,128)(2,1)S(1)}, bf16[12,64,1024]{2,1,0:T(8,128)(2,1)}, u32[]{:S(2)}, u32[]{:S(2)}) collective-permute-start(bf16[12,64,1024]{2,1,0:T(8,128)(2,1)S(1)} %bitcast.26), channel_id=1, source_target_pairs={{0,16},{4,20},{8,24},{12,28},{16,0},{20,4},{24,8},{28,12},{1,17},{... | collective-permute-start | bytes 4718600 | tf_op jit(solution)/shard_map/ppermute | solution.py:121
  23.1 0.5 collective-permute-start.3
  23.7 0.0 collective-permute-start.2
  23.7 34.8 %collective-permute-done.7.rest_6_ = bf16[12,64,1024]{2,1,0:T(8,128)(2,1)} collective-permute-done((bf16[12,64,1024]{2,1,0:T(8,128)(2,1)S(1)}, bf16[12,64,1024]{2,1,0:T(8,128)(2,1)}, u32[]{:S(2)}, u32[]{:S(2)}) %collective-permute-start.7) | collective-permute-done | bytes 1572896 | tf_op jit(solution)/shard_map/ppermute | solution.py:121
  58.5 0.0 collective-permute-start.8
  58.5 31.3 %collective-permute-done.5.rest_4_ = bf16[12,64,1024]{2,1,0:T(8,128)(2,1)} collective-permute-done((bf16[12,64,1024]{2,1,0:T(8,128)(2,1)S(1)}, bf16[12,64,1024]{2,1,0:T(8,128)(2,1)}, u32[]{:S(2)}, u32[]{:S(2)}) %collective-permute-start.5) | collective-permute-done | bytes 1572896 | tf_op jit(solution)/shard_map/ppermute | solution.py:121
  89.8 0.0 collective-permute-start.6
  89.8 0.0 collective-permute-done.3.rest_2_
  89.8 0.5 collective-permute-start.4
  90.3 0.0 copy-done.1
  90.4 0.1 copy.7
  90.5 0.1 reshape.215.where_ref
  90.6 0.0 copy-done.2
  90.6 0.0 collective-permute-done.2.rest_1_
  90.6 0.0 collective-permute-done.8.rest_7_
  90.7 5.0 %collective-permute-done.6.rest_5_ = bf16[12,64,1024]{2,1,0:T(8,128)(2,1)} collective-permute-done((bf16[12,64,1024]{2,1,0:T(8,128)(2,1)}, bf16[12,64,1024]{2,1,0:T(8,128)(2,1)}, u32[]{:S(2)}, u32[]{:S(2)}) %collective-permute-start.6) | collective-permute-done | bytes 1572896 | tf_op jit(solution)/shard_map/ppermute | solution.py:121
  95.6 0.0 collective-permute-done.4.rest_3_
  95.6 0.0 copy-done
  95.6 18.9 %shard_map.55 = bf16[128,1024]{1,0:T(8,128)(2,1)} custom-call(s32[128]{0:T(128)S(1)} %reshape.215.where_ref, s32[2]{0:T(128)S(1)} %clamp_bitcast_fusion.counts_ref, bf16[128,1024]{1,0:T(8,128)(2,1)S(1)} %bitcast.30, bf16[12,64,1024]{2,1,0:T(8,128)(2,1)S(1)} %bitcast.29, bf16[12,64,1024]{2,1,0:T(8,128)(2,1)} %collective-permute-done.2.rest_1_, ...), custom_call_target="tpu_custom_call" | custom-call | tf_op jit(solution)/shard_map/pallas_call | solution.py:111
  (3 shorter events, 0.0 us)
Async XLA Ops:
  1.1 89.3 %copy-start.1 = (s32[1,1,2,32]{3,2,1,0:T(2,128)S(1)}, s32[1,1,2,32]{3,2,1,0:T(2,128)}, u32[]{:S(2)}) copy-start(s32[1,1,2,32]{3,2,1,0:T(2,128)} %param.8) | copy-start | bytes 772
  1.1 89.5 %copy-start.2 = (s32[1,1,2]{2,1,0:T(1,128)S(1)}, s32[1,1,2]{2,1,0:T(1,128)}, u32[]{:S(2)}) copy-start(s32[1,1,2]{2,1,0:T(1,128)} %param.9) | copy-start | bytes 28
  1.1 94.5 %copy-start = (bf16[1,1,128,1024]{3,2,1,0:T(8,128)(2,1)S(1)}, bf16[1,1,128,1024]{3,2,1,0:T(8,128)(2,1)}, u32[]{:S(2)}) copy-start(bf16[1,1,128,1024]{3,2,1,0:T(8,128)(2,1)} %param.5) | copy-start | bytes 786436
  1.1 15.7 %collective-permute-start.1 = (bf16[2,1,1,128,1024]{4,3,2,1,0:T(8,128)(2,1)S(1)}, bf16[2,1,1,128,1024]{4,3,2,1,0:T(8,128)(2,1)S(1)}, u32[]{:S(2)}, u32[]{:S(2)}) collective-permute-start(bf16[2,1,1,128,1024]{4,3,2,1,0:T(8,128)(2,1)S(1)} %pad_maximum_fusion.1), channel_id=1, source_target_pairs={{1,0},{2,1},{3,2},{5,4},{6,5},{7,6},{9,8},{10,9},{11,10},{13,12},{... | collective-permute-start | bytes 1572872 | tf_op jit(solution)/shard_map/ppermute | solution.py:26
  3.6 15.3 %collective-permute-start = (bf16[2,1,1,128,1024]{4,3,2,1,0:T(8,128)(2,1)S(1)}, bf16[2,1,1,128,1024]{4,3,2,1,0:T(8,128)(2,1)S(1)}, u32[]{:S(2)}, u32[]{:S(2)}) collective-permute-start(bf16[2,1,1,128,1024]{4,3,2,1,0:T(8,128)(2,1)S(1)} %pad_maximum_fusion.1), channel_id=1, source_target_pairs={{0,1},{1,2},{2,3},{4,5},{5,6},{6,7},{8,9},{9,10},{10,11},{12,13},{... | collective-permute-start | bytes 1572872 | tf_op jit(solution)/shard_map/ppermute | solution.py:24
  20.1 38.4 %collective-permute-start.7 = (bf16[12,64,1024]{2,1,0:T(8,128)(2,1)S(1)}, bf16[12,64,1024]{2,1,0:T(8,128)(2,1)}, u32[]{:S(2)}, u32[]{:S(2)}) collective-permute-start(bf16[12,64,1024]{2,1,0:T(8,128)(2,1)S(1)} %bitcast.25), channel_id=1, source_target_pairs={{0,24},{4,28},{8,16},{12,20},{16,8},{20,12},{24,0},{28,4},{1,25},{... | collective-permute-start | bytes 4718600 | tf_op jit(solution)/shard_map/ppermute | solution.py:121
  21.6 68.2 %collective-permute-start.5 = (bf16[12,64,1024]{2,1,0:T(8,128)(2,1)S(1)}, bf16[12,64,1024]{2,1,0:T(8,128)(2,1)}, u32[]{:S(2)}, u32[]{:S(2)}) collective-permute-start(bf16[12,64,1024]{2,1,0:T(8,128)(2,1)S(1)} %bitcast.26), channel_id=1, source_target_pairs={{0,16},{4,20},{8,24},{12,28},{16,0},{20,4},{24,8},{28,12},{1,17},{... | collective-permute-start | bytes 4718600 | tf_op jit(solution)/shard_map/ppermute | solution.py:121
  23.1 66.7 %collective-permute-start.3 = (bf16[12,64,1024]{2,1,0:T(8,128)(2,1)S(1)}, bf16[12,64,1024]{2,1,0:T(8,128)(2,1)S(1)}, u32[]{:S(2)}, u32[]{:S(2)}) collective-permute-start(bf16[12,64,1024]{2,1,0:T(8,128)(2,1)S(1)} %bitcast.27), channel_id=1, source_target_pairs={{0,8},{4,12},{8,0},{12,4},{16,24},{20,28},{24,16},{28,20},{1,9},{5... | collective-permute-start | bytes 4718600 | tf_op jit(solution)/shard_map/ppermute | solution.py:121
  23.7 67.0 %collective-permute-start.2 = (bf16[12,64,1024]{2,1,0:T(8,128)(2,1)S(1)}, bf16[12,64,1024]{2,1,0:T(8,128)(2,1)}, u32[]{:S(2)}, u32[]{:S(2)}) collective-permute-start(bf16[12,64,1024]{2,1,0:T(8,128)(2,1)S(1)} %bitcast.28), channel_id=1, source_target_pairs={{0,4},{4,0},{8,12},{12,8},{16,20},{20,16},{24,28},{28,24},{1,5},{5... | collective-permute-start | bytes 4718600 | tf_op jit(solution)/shard_map/ppermute | solution.py:121
  58.5 32.1 %collective-permute-start.8 = (bf16[12,64,1024]{2,1,0:T(8,128)(2,1)}, bf16[12,64,1024]{2,1,0:T(8,128)(2,1)}, u32[]{:S(2)}, u32[]{:S(2)}) collective-permute-start(bf16[12,64,1024]{2,1,0:T(8,128)(2,1)} %collective-permute-done.7.rest_6_), channel_id=1, source_target_pairs={{0,4},{4,0},{8,12},{12,8},{16,20},{20,16},{24,28},{28,24},{1,5},{5... | collective-permute-start | bytes 4718600 | tf_op jit(solution)/shard_map/ppermute | solution.py:121
  89.8 5.8 %collective-permute-start.6 = (bf16[12,64,1024]{2,1,0:T(8,128)(2,1)}, bf16[12,64,1024]{2,1,0:T(8,128)(2,1)}, u32[]{:S(2)}, u32[]{:S(2)}) collective-permute-start(bf16[12,64,1024]{2,1,0:T(8,128)(2,1)} %collective-permute-done.5.rest_4_), channel_id=1, source_target_pairs={{0,4},{4,0},{8,12},{12,8},{16,20},{20,16},{24,28},{28,24},{1,5},{5... | collective-permute-start | bytes 4718600 | tf_op jit(solution)/shard_map/ppermute | solution.py:121
  89.8 5.8 %collective-permute-start.4 = (bf16[12,64,1024]{2,1,0:T(8,128)(2,1)S(1)}, bf16[12,64,1024]{2,1,0:T(8,128)(2,1)}, u32[]{:S(2)}, u32[]{:S(2)}) collective-permute-start(bf16[12,64,1024]{2,1,0:T(8,128)(2,1)S(1)} %collective-permute-done.3.rest_2_), channel_id=1, source_target_pairs={{0,4},{4,0},{8,12},{12,8},{16,20},{20,16},{24,28},{28,24},{1,5},{5... | collective-permute-start | bytes 4718600 | tf_op jit(solution)/shard_map/ppermute | solution.py:121
where the time goes:
time: 115 us; the launch traced here: 114 us
  waiting for transfers between devices  82.9 us (72%)
  Pallas kernels  18.9 us (16%)
  starting transfers between devices  10.1 us (9%)
  other arithmetic  2.31 us (2%)
    ppermute x7, waiting for transfers between devices, swap(): return lax.ppermute(piece, 'tm', [(i, i ^ mask) for i in range(count)])  71.1 us
    pallas_call x1, Pallas kernels, attend(): pl.pallas_call(kernel, grid_spec=grid_spec, out_shape=jax.ShapeDtypeStruc...  18.9 us
    ppermute x1, waiting for transfers between devices, with_halo(): lax.ppermute(head, axis, [((i + 1) % count, i) for i in range(ends)])  9.67 us
    ppermute x7, starting transfers between devices, swap(): return lax.ppermute(piece, 'tm', [(i, i ^ mask) for i in range(count)])  4.07 us
    ppermute x1, starting transfers between devices, with_halo(): lax.ppermute(tail, axis, [(i, (i + 1) % count) for i in range(ends)])  3.51 us
    ppermute x1, starting transfers between devices, with_halo(): lax.ppermute(head, axis, [((i + 1) % count, i) for i in range(ends)])  2.49 us
  transfers between devices with their start and end apart: 9, of which 5 were waited for; matrix products, arithmetic and copies ran while one was open for 0% of the time, Pallas kernels for 0%

commit v1 on v0

v1 whole, which is shorter than its diff:
```python
import functools

import jax
import jax.numpy as jnp
from jax import lax
from jax.experimental import pallas as pl
from jax.experimental.pallas import tpu as pltpu
from jax.sharding import PartitionSpec as P

HEADS = 8
HDIM = 128
BLOCK = 64
PICKS = 32


def dispatch(index, low, high, act):
    if high - low == 1:
        act(low)
        return
    middle = (low + high) // 2

    @pl.when(index < middle)
    def _():
        dispatch(index, low, middle, act)

    @pl.when(index >= middle)
    def _():
        dispatch(index, middle, high, act)


def attend_kernel(where_ref, counts_ref, q_ref, *rest, blocks_here, pieces):
    sources = rest[:pieces]
    o_ref, kvbuf, sems = rest[pieces:]
    feature_width = q_ref.shape[1]

    def copy(qb, p, source):
        row = where_ref[2 * (qb * PICKS + p) + 1]
        return pltpu.make_async_copy(source.at[row], kvbuf.at[qb, p], sems.at[qb, p])

    for qb in range(blocks_here):
        count = counts_ref[qb]

        def start(p, carry, qb=qb):
            piece = where_ref[2 * (qb * PICKS + p)]

            def act(j):
                copy(qb, p, sources[j]).start()

            dispatch(piece, 0, pieces, act)
            return carry

        def clear(p, carry, qb=qb):
            kvbuf[qb, p, 1] = jnp.zeros((BLOCK, feature_width), kvbuf.dtype)
            return carry

        lax.fori_loop(0, count, start, 0)
        lax.fori_loop(count, PICKS, clear, 0)

    for qb in range(blocks_here):
        count = counts_ref[qb]

        def finish(p, carry, qb=qb):
            copy(qb, p, sources[0]).wait()
            return carry

        lax.fori_loop(0, count, finish, 0)
        column = lax.broadcasted_iota(jnp.int32, (BLOCK, PICKS * BLOCK), 1)
        usable = column < count * BLOCK
        for h in range(HEADS):
            cols = slice(h * HDIM, (h + 1) * HDIM)
            q_h = q_ref[qb * BLOCK:(qb + 1) * BLOCK, cols]
            k_h = kvbuf[qb, :, 0, :, cols].reshape(PICKS * BLOCK, HDIM)
            v_h = kvbuf[qb, :, 1, :, cols].reshape(PICKS * BLOCK, HDIM)
            scores = lax.dot_general(
                q_h, k_h, (((1,), (1,)), ((), ())), preferred_element_type=jnp.float32
            ) * HDIM ** (-0.5)
            scores = jnp.where(usable, scores, -1e30)
            peaks = jnp.max(scores, axis=-1, keepdims=True)
            weights = jnp.exp(scores - peaks)
            totals = jnp.sum(weights, axis=-1, keepdims=True)
            rounded = weights.astype(jnp.bfloat16)
            blended = jnp.dot(rounded, v_h, preferred_element_type=jnp.float32)
            o_ref[qb * BLOCK:(qb + 1) * BLOCK, cols] = (blended / totals).astype(o_ref.dtype)


def attend(query_rows, sources, where, counts):
    tokens_here, feature_width = query_rows.shape
    blocks_here = tokens_here // BLOCK
    kernel = functools.partial(attend_kernel, blocks_here=blocks_here, pieces=len(sources))
    grid_spec = pltpu.PrefetchScalarGridSpec(
        num_scalar_prefetch=2,
        grid=(1,),
        in_specs=[pl.BlockSpec((tokens_here, feature_width), lambda i, w, c: (0, 0))]
        + [pl.BlockSpec(memory_space=pl.ANY) for _ in sources],
        out_specs=pl.BlockSpec((tokens_here, feature_width), lambda i, w, c: (0, 0)),
        scratch_shapes=[
            pltpu.VMEM((blocks_here, PICKS, 2, BLOCK, feature_width), query_rows.dtype),
            pltpu.SemaphoreType.DMA((blocks_here, PICKS)),
        ],
    )
    return pl.pallas_call(
        kernel,
        grid_spec=grid_spec,
        out_shape=jax.ShapeDtypeStruct((tokens_here, feature_width), query_rows.dtype),
        compiler_params=pltpu.CompilerParams(vmem_limit_bytes=48 * 1024 * 1024),
    )(where, counts, query_rows, *sources)


def swap(piece, mask):
    count = lax.axis_size("tm")
    return lax.ppermute(piece, "tm", [(i, i ^ mask) for i in range(count)])


def exchange(own, masks):
    pieces = {0: own}
    for mask in masks:
        if mask % 2 == 0 and mask > 0:
            pieces[mask] = swap(own, mask)
    for mask in masks:
        if mask % 2 == 1:
            pieces[mask] = swap(pieces[mask - 1], 1)
    return [pieces[mask] for mask in masks]


def on_device(queries, key_vectors, value_vectors, key_blocks, block_count):
    groups_here = queries.shape[0]
    tokens_here = queries.shape[2]
    feature_width = queries.shape[3]
    blocks_here = tokens_here // BLOCK
    members = lax.axis_size("tm")
    assert members & (members - 1) == 0 and members % 2 == 0
    far = members - 2
    split = (groups_here, 1, blocks_here, BLOCK, feature_width)
    stacked = jnp.stack([key_vectors.reshape(split), value_vectors.reshape(split)], axis=3)
    per_band = groups_here * blocks_here
    gathered = lax.all_gather(stacked, "tm", axis=0, tiled=True)
    gathered = gathered.reshape(members * per_band, 2, BLOCK, feature_width)
    me = lax.axis_index("tm")
    far_piece = lax.dynamic_slice_in_dim(gathered, jnp.bitwise_xor(me, far) * per_band, per_band, axis=0)
    count = lax.axis_size("space")
    ends = count - 1
    up = [(i, i + 1) for i in range(ends)]
    down = [(i + 1, i) for i in range(ends)]
    below = lax.ppermute(stacked, "space", up)
    above = lax.ppermute(stacked, "space", down)
    halo = jnp.concatenate([below, above], axis=1)
    sides = exchange(halo.reshape(2 * per_band, 2, BLOCK, feature_width), list(range(far)))
    from_below = lax.ppermute(far_piece, "space", up)
    from_above = lax.ppermute(far_piece, "space", down)
    relayed = [from_below, swap(from_below, 1), from_above, swap(from_above, 1)]
    own_band = lax.axis_index("space")
    listed = key_blocks.reshape(blocks_here, PICKS)
    within = listed % blocks_here
    band_of = listed // blocks_here % count
    group_of = jnp.clip(listed // (blocks_here * count), 0, members * groups_here - 1)
    holder = group_of // groups_here
    shift = band_of - own_band
    mask = jnp.bitwise_xor(holder, me)
    piece = jnp.where(shift == 0, 0, 1 + mask + jnp.where((mask >= far) & (shift > 0), 2, 0))
    local = group_of % groups_here
    side = jnp.where(shift < 0, 0, 1)
    row = jnp.where((shift == 0) | (mask >= far), local, local * 2 + side) * blocks_here + within
    row = jnp.where(shift == 0, holder * per_band + row, row)
    where = jnp.stack([piece, row], axis=-1).reshape(-1).astype(jnp.int32)
    counts = jnp.clip(block_count.reshape(blocks_here), 1, PICKS).astype(jnp.int32)
    sources = [gathered] + sides + relayed
    result = attend(queries.reshape(tokens_here, feature_width), sources, where, counts)
    return result.reshape(queries.shape)


def solution(mesh):
    in_specs = (
        P("tm", "space", None, None),
        P("tm", "space", None, None),
        P("tm", "space", None, None),
        P("tm", "space", None, None),
        P("tm", "space", None),
    )
    out_specs = P("tm", "space", None, None)
    return jax.shard_map(
        on_device, mesh=mesh, in_specs=in_specs, out_specs=out_specs, check_vma=False
    )
```

time: 115 us -> 102 us (0.89)
  the two profiles are of different devices: /device:TPU:20 before, /device:TPU:0 now
where the time goes in v1:
time: 102 us; the launch traced here: 101 us
  waiting for transfers between devices  53.5 us (52%)
  starting transfers between devices  17.3 us (17%)
  between operations  13.5 us (13%)
  Pallas kernels  12.2 us (12%)
  local copies, waits for them, and re-layouts  2.13 us (2%)
  other arithmetic  2.1 us (2%)
    all_gather x1, waiting for transfers between devices, on_device(): gathered = lax.all_gather(stacked, 'tm', axis=0, tiled=True)  29.9 us
    pallas_call x1, Pallas kernels, attend(): pl.pallas_call(kernel, grid_spec=grid_spec, out_shape=jax.ShapeDtypeStruc...  12.2 us
    ppermute x1, waiting for transfers between devices, on_device(): above = lax.ppermute(stacked, 'space', down)  10.2 us
    ppermute x1, waiting for transfers between devices, on_device(): from_above = lax.ppermute(far_piece, 'space', down)  9.04 us
    ppermute x1, starting transfers between devices, on_device(): below = lax.ppermute(stacked, 'space', up)  5.59 us
    ppermute x1, starting transfers between devices, on_device(): from_below = lax.ppermute(far_piece, 'space', up)  5.35 us
    ppermute x7, starting transfers between devices, swap(): return lax.ppermute(piece, 'tm', [(i, i ^ mask) for i in range(count)])  3.82 us
  transfers between devices with their start and end apart: 12, of which 7 were waited for; matrix products, arithmetic and copies ran while one was open for 2% of the time, Pallas kernels for 0%

profile of v1, /device:TPU:0, one launch (start us, length us, event | category | flops | bytes accessed | tf_op | source)
XLA Modules:
  0.0 100.8 jit_solution(9352502024400456649)
XLA Ops:
  6.5 0.0 all-gather.2.cloned.1.call-start
  6.5 2.0 %pad_maximum_fusion.1 = bf16[1,1,2,2,64,1024]{5,4,3,2,1,0:T(8,128)(2,1)} fusion(bf16[1,1,2,1,64,1024]{5,4,3,2,1,0:T(8,128)(2,1)} %bitcast.42, bf16[1,1,2,1,64,1024]{5,4,3,2,1,0:T(8,128)(2,1)} %bitcast.43), kind=kLoop, calls=%fused_computation.1 | loop fusion | flops 262144 | bytes 1048576 | tf_op jit(solution)/shard_map/stack | solution.py:134
  8.5 0.0 all-gather.2.cloned.1.call-update
  8.5 1.3 %collective-permute-start.1 = (bf16[1,1,2,2,64,1024]{5,4,3,2,1,0:T(8,128)(2,1)}, bf16[1,1,2,2,64,1024]{5,4,3,2,1,0:T(8,128)(2,1)S(1)}, u32[]{:S(2)}, u32[]{:S(2)}) collective-permute-start(bf16[1,1,2,2,64,1024]{5,4,3,2,1,0:T(8,128)(2,1)} %pad_maximum_fusion.1), channel_id=1, source_target_pairs={{1,0},{2,1},{3,2},{5,4},{6,5},{7,6},{9,8},{10,9},{11,10},{13,12},{... | collective-permute-start | bytes 1572872 | tf_op jit(solution)/shard_map/ppermute | solution.py:145
  9.8 5.6 %collective-permute-start = (bf16[1,1,2,2,64,1024]{5,4,3,2,1,0:T(8,128)(2,1)}, bf16[1,1,2,2,64,1024]{5,4,3,2,1,0:T(8,128)(2,1)S(1)}, u32[]{:S(2)}, u32[]{:S(2)}) collective-permute-start(bf16[1,1,2,2,64,1024]{5,4,3,2,1,0:T(8,128)(2,1)} %pad_maximum_fusion.1), channel_id=1, source_target_pairs={{0,1},{1,2},{2,3},{4,5},{5,6},{6,7},{8,9},{9,10},{10,11},{12,13},{... | collective-permute-start | bytes 1572872 | tf_op jit(solution)/shard_map/ppermute | solution.py:144
  15.4 10.2 %collective-permute-done.1 = bf16[1,1,2,2,64,1024]{5,4,3,2,1,0:T(8,128)(2,1)S(1)} collective-permute-done((bf16[1,1,2,2,64,1024]{5,4,3,2,1,0:T(8,128)(2,1)}, bf16[1,1,2,2,64,1024]{5,4,3,2,1,0:T(8,128)(2,1)S(1)}, u32[]{:S(2)}, u32[]{:S(2)}) %collective-permute-start.1) | collective-permute-done | bytes 524320 | tf_op jit(solution)/shard_map/ppermute | solution.py:145
  25.6 1.3 %collective-permute-done = bf16[1,1,2,2,64,1024]{5,4,3,2,1,0:T(8,128)(2,1)S(1)} collective-permute-done((bf16[1,1,2,2,64,1024]{5,4,3,2,1,0:T(8,128)(2,1)}, bf16[1,1,2,2,64,1024]{5,4,3,2,1,0:T(8,128)(2,1)S(1)}, u32[]{:S(2)}, u32[]{:S(2)}) %collective-permute-start) | collective-permute-done | bytes 524320 | tf_op jit(solution)/shard_map/ppermute | solution.py:144
  26.9 0.1 pad_maximum_fusion
  27.0 1.7 %collective-permute-start.5 = (bf16[4,2,64,1024]{3,2,1,0:T(8,128)(2,1)S(1)}, bf16[4,2,64,1024]{3,2,1,0:T(8,128)(2,1)}, u32[]{:S(2)}, u32[]{:S(2)}) collective-permute-start(bf16[4,2,64,1024]{3,2,1,0:T(8,128)(2,1)S(1)} %bitcast.35), channel_id=1, source_target_pairs={{0,16},{4,20},{8,24},{12,28},{16,0},{20,4},{24,8},{28,12},{1,17},{... | collective-permute-start | bytes 3145736 | tf_op jit(solution)/shard_map/ppermute | solution.py:111
  28.7 1.5 %collective-permute-start.3 = (bf16[4,2,64,1024]{3,2,1,0:T(8,128)(2,1)S(1)}, bf16[4,2,64,1024]{3,2,1,0:T(8,128)(2,1)S(1)}, u32[]{:S(2)}, u32[]{:S(2)}) collective-permute-start(bf16[4,2,64,1024]{3,2,1,0:T(8,128)(2,1)S(1)} %bitcast.36), channel_id=1, source_target_pairs={{0,8},{4,12},{8,0},{12,4},{16,24},{20,28},{24,16},{28,20},{1,9},{5... | collective-permute-start | bytes 3145736 | tf_op jit(solution)/shard_map/ppermute | solution.py:111
  30.2 29.9 %all-gather.2.cloned.1.call-done = bf16[8,1,2,2,64,1024]{5,4,3,2,1,0:T(8,128)(2,1)} async-done(((bf16[1,1,2,2,64,1024]{5,4,3,2,1,0:T(8,128)(2,1)}), bf16[8,1,2,2,64,1024]{5,4,3,2,1,0:T(8,128)(2,1)}) %all-gather.2.cloned.1.call-update) | async-done | bytes 4194320 | tf_op jit(solution)/shard_map/all_gather | solution.py:136
  60.1 1.9 %constant_dynamic-slice_fusion = bf16[2,2,64,1024]{3,2,1,0:T(8,128)(2,1)} fusion(bf16[16,2,64,1024]{3,2,1,0:T(8,128)(2,1)} %bitcast.40, s32[]{:T(128)S(6)} %select_n.132), kind=kLoop, calls=%fused_computation.31 | loop fusion | bytes 1048580 | tf_op jit(solution)/shard_map/dynamic_slice | solution.py:139
  61.9 1.3 %collective-permute-start.9 = (bf16[2,2,64,1024]{3,2,1,0:T(8,128)(2,1)}, bf16[2,2,64,1024]{3,2,1,0:T(8,128)(2,1)}, u32[]{:S(2)}, u32[]{:S(2)}) collective-permute-start(bf16[2,2,64,1024]{3,2,1,0:T(8,128)(2,1)} %constant_dynamic-slice_fusion), channel_id=1, source_target_pairs={{1,0},{2,1},{3,2},{5,4},{6,5},{7,6},{9,8},{10,9},{11,10},{13,12},{... | collective-permute-start | bytes 1572872 | tf_op jit(solution)/shard_map/ppermute | solution.py:149
  63.2 5.3 %collective-permute-start.7 = (bf16[2,2,64,1024]{3,2,1,0:T(8,128)(2,1)}, bf16[2,2,64,1024]{3,2,1,0:T(8,128)(2,1)}, u32[]{:S(2)}, u32[]{:S(2)}) collective-permute-start(bf16[2,2,64,1024]{3,2,1,0:T(8,128)(2,1)} %constant_dynamic-slice_fusion), channel_id=1, source_target_pairs={{0,1},{1,2},{2,3},{4,5},{5,6},{6,7},{8,9},{9,10},{10,11},{12,13},{... | collective-permute-start | bytes 1572872 | tf_op jit(solution)/shard_map/ppermute | solution.py:148
  68.6 0.0 collective-permute-start.2
  68.6 0.0 collective-permute-done.5.rest_5_
  68.6 0.5 collective-permute-start.6
  69.1 0.0 collective-permute-done.3.rest_3_
  69.1 0.1 collective-permute-start.4
  69.2 0.0 copy-done.1
  69.2 9.0 %collective-permute-done.9.rest_9_ = bf16[2,2,64,1024]{3,2,1,0:T(8,128)(2,1)} collective-permute-done((bf16[2,2,64,1024]{3,2,1,0:T(8,128)(2,1)}, bf16[2,2,64,1024]{3,2,1,0:T(8,128)(2,1)}, u32[]{:S(2)}, u32[]{:S(2)}) %collective-permute-start.9) | collective-permute-done | bytes 524320 | tf_op jit(solution)/shard_map/ppermute | solution.py:149
  78.2 0.0 collective-permute-start.10
  78.2 1.2 %collective-permute-done.7.rest_7_ = bf16[2,2,64,1024]{3,2,1,0:T(8,128)(2,1)} collective-permute-done((bf16[2,2,64,1024]{3,2,1,0:T(8,128)(2,1)}, bf16[2,2,64,1024]{3,2,1,0:T(8,128)(2,1)}, u32[]{:S(2)}, u32[]{:S(2)}) %collective-permute-start.7) | collective-permute-done | bytes 524320 | tf_op jit(solution)/shard_map/ppermute | solution.py:148
  79.4 0.0 collective-permute-start.8
  79.4 0.1 copy.12
  79.5 0.1 reshape.257.where_ref
  79.7 0.0 collective-permute-done.2.rest_2_
  79.7 0.0 collective-permute-done.6.rest_6_
  79.7 0.0 collective-permute-done.4.rest_4_
  79.7 0.7 collective-permute-done.10.rest_10_
  80.5 1.2 %collective-permute-done.8.rest_8_ = bf16[2,2,64,1024]{3,2,1,0:T(8,128)(2,1)} collective-permute-done((bf16[2,2,64,1024]{3,2,1,0:T(8,128)(2,1)}, bf16[2,2,64,1024]{3,2,1,0:T(8,128)(2,1)}, u32[]{:S(2)}, u32[]{:S(2)}) %collective-permute-start.8) | collective-permute-done | bytes 524320 | tf_op jit(solution)/shard_map/ppermute | solution.py:111
  81.7 12.2 %shard_map.55 = bf16[128,1024]{1,0:T(8,128)(2,1)} custom-call(s32[128]{0:T(128)S(1)} %reshape.257.where_ref, s32[2]{0:T(128)S(1)} %clamp_bitcast_fusion.counts_ref, bf16[128,1024]{1,0:T(8,128)(2,1)S(1)} %bitcast.39, bf16[16,2,64,1024]{3,2,1,0:T(8,128)(2,1)} %bitcast.41, bf16[4,2,64,1024]{3,2,1,0:T(8,128)(2,1)S(1)} %bitcast.38, ...), custom_call_target="tpu_custom_call" | custom-call | tf_op jit(solution)/shard_map/pallas_call | solution.py:101
  (9 shorter events, 0.1 us)
Async XLA Ops:
  6.5 62.6 %copy-start.1 = (s32[1,1,2,32]{3,2,1,0:T(2,128)S(1)}, s32[1,1,2,32]{3,2,1,0:T(2,128)}, u32[]{:S(2)}) copy-start(s32[1,1,2,32]{3,2,1,0:T(2,128)} %param.8) | copy-start | bytes 772
  6.5 73.2 %copy-start.2 = (s32[1,1,2]{2,1,0:T(1,128)S(1)}, s32[1,1,2]{2,1,0:T(1,128)}, u32[]{:S(2)}) copy-start(s32[1,1,2]{2,1,0:T(1,128)} %param.9) | copy-start | bytes 28
  6.5 75.1 %copy-start = (bf16[1,1,128,1024]{3,2,1,0:T(8,128)(2,1)S(1)}, bf16[1,1,128,1024]{3,2,1,0:T(8,128)(2,1)}, u32[]{:S(2)}) copy-start(bf16[1,1,128,1024]{3,2,1,0:T(8,128)(2,1)} %param.5) | copy-start | bytes 786436
  6.5 53.5 %all-gather.2.cloned.1.call-start = ((), (), s32[]{:S(2)}) async-start(), calls=%async_computation | async-start | bytes 4718592 | tf_op jit(solution)/shard_map/all_gather | solution.py:136
  8.5 17.1 %collective-permute-start.1 = (bf16[1,1,2,2,64,1024]{5,4,3,2,1,0:T(8,128)(2,1)}, bf16[1,1,2,2,64,1024]{5,4,3,2,1,0:T(8,128)(2,1)S(1)}, u32[]{:S(2)}, u32[]{:S(2)}) collective-permute-start(bf16[1,1,2,2,64,1024]{5,4,3,2,1,0:T(8,128)(2,1)} %pad_maximum_fusion.1), channel_id=1, source_target_pairs={{1,0},{2,1},{3,2},{5,4},{6,5},{7,6},{9,8},{10,9},{11,10},{13,12},{... | collective-permute-start | bytes 1572872 | tf_op jit(solution)/shard_map/ppermute | solution.py:145
  9.8 17.0 %collective-permute-start = (bf16[1,1,2,2,64,1024]{5,4,3,2,1,0:T(8,128)(2,1)}, bf16[1,1,2,2,64,1024]{5,4,3,2,1,0:T(8,128)(2,1)S(1)}, u32[]{:S(2)}, u32[]{:S(2)}) collective-permute-start(bf16[1,1,2,2,64,1024]{5,4,3,2,1,0:T(8,128)(2,1)} %pad_maximum_fusion.1), channel_id=1, source_target_pairs={{0,1},{1,2},{2,3},{4,5},{5,6},{6,7},{8,9},{9,10},{10,11},{12,13},{... | collective-permute-start | bytes 1572872 | tf_op jit(solution)/shard_map/ppermute | solution.py:144
  27.0 41.6 %collective-permute-start.5 = (bf16[4,2,64,1024]{3,2,1,0:T(8,128)(2,1)S(1)}, bf16[4,2,64,1024]{3,2,1,0:T(8,128)(2,1)}, u32[]{:S(2)}, u32[]{:S(2)}) collective-permute-start(bf16[4,2,64,1024]{3,2,1,0:T(8,128)(2,1)S(1)} %bitcast.35), channel_id=1, source_target_pairs={{0,16},{4,20},{8,24},{12,28},{16,0},{20,4},{24,8},{28,12},{1,17},{... | collective-permute-start | bytes 3145736 | tf_op jit(solution)/shard_map/ppermute | solution.py:111
  28.7 40.4 %collective-permute-start.3 = (bf16[4,2,64,1024]{3,2,1,0:T(8,128)(2,1)S(1)}, bf16[4,2,64,1024]{3,2,1,0:T(8,128)(2,1)S(1)}, u32[]{:S(2)}, u32[]{:S(2)}) collective-permute-start(bf16[4,2,64,1024]{3,2,1,0:T(8,128)(2,1)S(1)} %bitcast.36), channel_id=1, source_target_pairs={{0,8},{4,12},{8,0},{12,4},{16,24},{20,28},{24,16},{28,20},{1,9},{5... | collective-permute-start | bytes 3145736 | tf_op jit(solution)/shard_map/ppermute | solution.py:111
  61.9 16.3 %collective-permute-start.9 = (bf16[2,2,64,1024]{3,2,1,0:T(8,128)(2,1)}, bf16[2,2,64,1024]{3,2,1,0:T(8,128)(2,1)}, u32[]{:S(2)}, u32[]{:S(2)}) collective-permute-start(bf16[2,2,64,1024]{3,2,1,0:T(8,128)(2,1)} %constant_dynamic-slice_fusion), channel_id=1, source_target_pairs={{1,0},{2,1},{3,2},{5,4},{6,5},{7,6},{9,8},{10,9},{11,10},{13,12},{... | collective-permute-start | bytes 1572872 | tf_op jit(solution)/shard_map/ppermute | solution.py:149
  63.2 16.2 %collective-permute-start.7 = (bf16[2,2,64,1024]{3,2,1,0:T(8,128)(2,1)}, bf16[2,2,64,1024]{3,2,1,0:T(8,128)(2,1)}, u32[]{:S(2)}, u32[]{:S(2)}) collective-permute-start(bf16[2,2,64,1024]{3,2,1,0:T(8,128)(2,1)} %constant_dynamic-slice_fusion), channel_id=1, source_target_pairs={{0,1},{1,2},{2,3},{4,5},{5,6},{6,7},{8,9},{9,10},{10,11},{12,13},{... | collective-permute-start | bytes 1572872 | tf_op jit(solution)/shard_map/ppermute | solution.py:148
  68.6 11.1 %collective-permute-start.2 = (bf16[4,2,64,1024]{3,2,1,0:T(8,128)(2,1)S(1)}, bf16[4,2,64,1024]{3,2,1,0:T(8,128)(2,1)S(1)}, u32[]{:S(2)}, u32[]{:S(2)}) collective-permute-start(bf16[4,2,64,1024]{3,2,1,0:T(8,128)(2,1)S(1)} %bitcast.37), channel_id=1, source_target_pairs={{0,4},{4,0},{8,12},{12,8},{16,20},{20,16},{24,28},{28,24},{1,5},{5... | collective-permute-start | bytes 3145736 | tf_op jit(solution)/shard_map/ppermute | solution.py:111
  68.6 11.1 %collective-permute-start.6 = (bf16[4,2,64,1024]{3,2,1,0:T(8,128)(2,1)}, bf16[4,2,64,1024]{3,2,1,0:T(8,128)(2,1)}, u32[]{:S(2)}, u32[]{:S(2)}) collective-permute-start(bf16[4,2,64,1024]{3,2,1,0:T(8,128)(2,1)} %collective-permute-done.5.rest_5_), channel_id=1, source_target_pairs={{0,4},{4,0},{8,12},{12,8},{16,20},{20,16},{24,28},{28,24},{1,5},{5... | collective-permute-start | bytes 3145736 | tf_op jit(solution)/shard_map/ppermute | solution.py:111
  69.1 10.6 %collective-permute-start.4 = (bf16[4,2,64,1024]{3,2,1,0:T(8,128)(2,1)S(1)}, bf16[4,2,64,1024]{3,2,1,0:T(8,128)(2,1)}, u32[]{:S(2)}, u32[]{:S(2)}) collective-permute-start(bf16[4,2,64,1024]{3,2,1,0:T(8,128)(2,1)S(1)} %collective-permute-done.3.rest_3_), channel_id=1, source_target_pairs={{0,4},{4,0},{8,12},{12,8},{16,20},{20,16},{24,28},{28,24},{1,5},{5... | collective-permute-start | bytes 3145736 | tf_op jit(solution)/shard_map/ppermute | solution.py:111
  78.2 2.3 %collective-permute-start.10 = (bf16[2,2,64,1024]{3,2,1,0:T(8,128)(2,1)}, bf16[2,2,64,1024]{3,2,1,0:T(8,128)(2,1)}, u32[]{:S(2)}, u32[]{:S(2)}) collective-permute-start(bf16[2,2,64,1024]{3,2,1,0:T(8,128)(2,1)} %collective-permute-done.9.rest_9_), channel_id=1, source_target_pairs={{0,4},{4,0},{8,12},{12,8},{16,20},{20,16},{24,28},{28,24},{1,5},{5... | collective-permute-start | bytes 1572872 | tf_op jit(solution)/shard_map/ppermute | solution.py:111
  79.4 2.3 %collective-permute-start.8 = (bf16[2,2,64,1024]{3,2,1,0:T(8,128)(2,1)}, bf16[2,2,64,1024]{3,2,1,0:T(8,128)(2,1)}, u32[]{:S(2)}, u32[]{:S(2)}) collective-permute-start(bf16[2,2,64,1024]{3,2,1,0:T(8,128)(2,1)} %collective-permute-done.7.rest_7_), channel_id=1, source_target_pairs={{0,4},{4,0},{8,12},{12,8},{16,20},{20,16},{24,28},{28,24},{1,5},{5... | collective-permute-start | bytes 1572872 | tf_op jit(solution)/shard_map/ppermute | solution.py:111
Sparse Core Ops, SparseCore 0:
  9.3 50.7 all-gather.1

commit v2 on v1

--- a/solution.py
+++ b/solution.py
@@ -133,22 +133,32 @@
     split = (groups_here, 1, blocks_here, BLOCK, feature_width)
     stacked = jnp.stack([key_vectors.reshape(split), value_vectors.reshape(split)], axis=3)
     per_band = groups_here * blocks_here
-    gathered = lax.all_gather(stacked, "tm", axis=0, tiled=True)
-    gathered = gathered.reshape(members * per_band, 2, BLOCK, feature_width)
-    me = lax.axis_index("tm")
-    far_piece = lax.dynamic_slice_in_dim(gathered, jnp.bitwise_xor(me, far) * per_band, per_band, axis=0)
+    tile = (per_band, 2, BLOCK, feature_width)
+    middle = exchange(stacked.reshape(tile), list(range(members)))
     count = lax.axis_size("space")
     ends = count - 1
-    up = [(i, i + 1) for i in range(ends)]
-    down = [(i + 1, i) for i in range(ends)]
-    below = lax.ppermute(stacked, "space", up)
-    above = lax.ppermute(stacked, "space", down)
-    halo = jnp.concatenate([below, above], axis=1)
-    sides = exchange(halo.reshape(2 * per_band, 2, BLOCK, feature_width), list(range(far)))
-    from_below = lax.ppermute(far_piece, "space", up)
-    from_above = lax.ppermute(far_piece, "space", down)
-    relayed = [from_below, swap(from_below, 1), from_above, swap(from_above, 1)]
+    toward = [[(i, i + 1) for i in range(ends)], [(i + 1, i) for i in range(ends)]]
+    bands = [lax.ppermute(stacked, "space", toward[d]).reshape(tile) for d in range(2)]
+    sources = list(middle)
+    table = [[None, None] for _ in range(members)]
+    for d in range(2):
+        for mask, piece in enumerate([bands[d], swap(bands[d], 1)]):
+            table[mask][d] = (len(sources), 0)
+            sources.append(piece)
+    for mask in range(2, members, 2):
+        direct = [] if mask == far else [(mask // 2 + 1) % 2]
+        for d in range(2):
+            if d in direct:
+                first = swap(bands[d], mask)
+            else:
+                first = lax.ppermute(middle[mask], "space", toward[d])
+            for j, piece in enumerate([first, swap(first, 1)]):
+                table[mask + j][d] = (len(sources), 0)
+                sources.append(piece)
+    lookup_piece = jnp.array([[table[m][d][0] for d in range(2)] for m in range(members)], jnp.int32)
+    lookup_base = jnp.array([[table[m][d][1] for d in range(2)] for m in range(members)], jnp.int32)
     own_band = lax.axis_index("space")
+    me = lax.axis_index("tm")
     listed = key_blocks.reshape(blocks_here, PICKS)
     within = listed % blocks_here
     band_of = listed // blocks_here % count
@@ -156,14 +166,12 @@
     holder = group_of // groups_here
     shift = band_of - own_band
     mask = jnp.bitwise_xor(holder, me)
-    piece = jnp.where(shift == 0, 0, 1 + mask + jnp.where((mask >= far) & (shift > 0), 2, 0))
-    local = group_of % groups_here
-    side = jnp.where(shift < 0, 0, 1)
-    row = jnp.where((shift == 0) | (mask >= far), local, local * 2 + side) * blocks_here + within
-    row = jnp.where(shift == 0, holder * per_band + row, row)
+    d = jnp.where(shift > 0, 1, 0)
+    local = (group_of % groups_here) * blocks_here + within
+    piece = jnp.where(shift == 0, mask, lookup_piece[mask, d])
+    row = jnp.where(shift == 0, local, lookup_base[mask, d] + local)
     where = jnp.stack([piece, row], axis=-1).reshape(-1).astype(jnp.int32)
     counts = jnp.clip(block_count.reshape(blocks_here), 1, PICKS).astype(jnp.int32)
-    sources = [gathered] + sides + relayed
     result = attend(queries.reshape(tokens_here, feature_width), sources, where, counts)
     return result.reshape(queries.shape)
 

time: 102 us -> 92.3 us (0.905)
  between operations: 13.5 us -> 0.13 us
  waiting for transfers between devices: 53.5 us -> 41.7 us
  starting transfers between devices: 17.3 us -> 25.7 us
  local copies, waits for them, and re-layouts: 2.13 us -> 9.32 us
    all_gather x1 -> x0, waiting for transfers between devices: 29.9 us -> none  [on_device(): gathered = lax.all_gather(stacked, 'tm', axis=0, tiled=True)]
    ppermute x7 -> x17, waiting for transfers between devices: 1.94 us -> 21.3 us  [swap(): return lax.ppermute(piece, 'tm', [(i, i ^ mask) for i in range(count)])]
    unnamed x6 -> x28, local copies, waits for them, and re-layouts: 0.01 us -> 7.38 us
    ppermute x7 -> x17, starting transfers between devices: 3.82 us -> 8.36 us  [swap(): return lax.ppermute(piece, 'tm', [(i, i ^ mask) for i in range(count)])]
    ppermute x4 -> x6, starting transfers between devices: 13.5 us -> 17.3 us  [the longest x4 11.1 us: on_device(): first = lax.ppermute(middle[mask], 'space', toward[d])]
    dynamic_slice x1 -> x0, local copies, waits for them, and re-layouts: 1.89 us -> none  [on_device(): lax.dynamic_slice_in_dim(gathered, jnp.bitwise_xor(me, far) * per_band, p...]
    gather x0 -> x4, local copies, waits for them, and re-layouts: none -> 1.63 us  [the longest x2 0.82 us: on_device(): row = jnp.where(shift == 0, local, lookup_base[mask, d] + local)]
    ppermute x4 -> x6, waiting for transfers between devices: 21.7 us -> 20.4 us  [the longest x2 10.4 us: on_device(): lax.ppermute(stacked, 'space', toward[d]).reshape(tile)]
  transfers between devices with their start and end apart: 12 -> 23, of which waited for: 7 -> 12; matrix products, arithmetic and copies ran while one was open for 2% -> 2% of each run, Pallas kernels for 0% -> 0%
where the time goes in v2:
time: 92.3 us; the launch traced here: 90.9 us
  waiting for transfers between devices  41.7 us (45%)
  starting transfers between devices  25.7 us (28%)
  Pallas kernels  13 us (14%)
  local copies, waits for them, and re-layouts  9.32 us (10%)
  other arithmetic  1.14 us (1%)
    ppermute x17, waiting for transfers between devices, swap(): return lax.ppermute(piece, 'tm', [(i, i ^ mask) for i in range(count)])  21.3 us
    pallas_call x1, Pallas kernels, attend(): pl.pallas_call(kernel, grid_spec=grid_spec, out_shape=jax.ShapeDtypeStruc...  13 us
    ppermute x4, starting transfers between devices, on_device(): first = lax.ppermute(middle[mask], 'space', toward[d])  11.1 us
    ppermute x2, waiting for transfers between devices, on_device(): lax.ppermute(stacked, 'space', toward[d]).reshape(tile)  10.4 us
    ppermute x4, waiting for transfers between devices, on_device(): first = lax.ppermute(middle[mask], 'space', toward[d])  9.99 us
    ppermute x17, starting transfers between devices, swap(): return lax.ppermute(piece, 'tm', [(i, i ^ mask) for i in range(count)])  8.36 us
    unnamed x28, local copies, waits for them, and re-layouts  7.38 us
    ppermute x2, starting transfers between devices, on_device(): lax.ppermute(stacked, 'space', toward[d]).reshape(tile)  6.25 us
  transfers between devices with their start and end apart: 23, of which 12 were waited for; matrix products, arithmetic and copies ran while one was open for 2% of the time, Pallas kernels for 0%

profile of v2, /device:TPU:0, one launch (start us, length us, event | category | flops | bytes accessed | tf_op | source)
XLA Modules:
  0.0 90.9 jit_solution(6935773887665596642)
XLA Ops:
  0.0 1.1 %pad_maximum_fusion = (bf16[1,1,2,2,64,1024]{5,4,3,2,1,0:T(8,128)(2,1)S(1)}, bf16[2,2,64,1024]{3,2,1,0:T(8,128)(2,1)S(1)}) fusion(bf16[1,1,2,1,64,1024]{5,4,3,2,1,0:T(8,128)(2,1)} %bitcast.43, bf16[1,1,2,1,64,1024]{5,4,3,2,1,0:T(8,128)(2,1)} %bitcast.44), kind=kLoop, calls=%fused_computation.2 | loop fusion | flops 262144 | bytes 1572864 | tf_op jit(solution)/shard_map/stack | solution.py:134
  1.1 5.0 %collective-permute-start.7 = (bf16[1,1,2,2,64,1024]{5,4,3,2,1,0:T(8,128)(2,1)S(1)}, bf16[1,1,2,2,64,1024]{5,4,3,2,1,0:T(8,128)(2,1)S(1)}, u32[]{:S(2)}, u32[]{:S(2)}) collective-permute-start(bf16[1,1,2,2,64,1024]{5,4,3,2,1,0:T(8,128)(2,1)S(1)} %get-tuple-element.8), channel_id=1, source_target_pairs={{0,1},{1,2},{2,3},{4,5},{5,6},{6,7},{8,9},{9,10},{10,11},{12,13},{... | collective-permute-start | bytes 1572872 | tf_op jit(solution)/shard_map/ppermute | solution.py:141
  6.1 1.3 %collective-permute-start.9 = (bf16[1,1,2,2,64,1024]{5,4,3,2,1,0:T(8,128)(2,1)S(1)}, bf16[1,1,2,2,64,1024]{5,4,3,2,1,0:T(8,128)(2,1)S(1)}, u32[]{:S(2)}, u32[]{:S(2)}) collective-permute-start(bf16[1,1,2,2,64,1024]{5,4,3,2,1,0:T(8,128)(2,1)S(1)} %get-tuple-element.8), channel_id=1, source_target_pairs={{1,0},{2,1},{3,2},{5,4},{6,5},{7,6},{9,8},{10,9},{11,10},{13,12},{... | collective-permute-start | bytes 1572872 | tf_op jit(solution)/shard_map/ppermute | solution.py:141
  7.4 2.5 %collective-permute-start.5 = (bf16[2,2,64,1024]{3,2,1,0:T(8,128)(2,1)S(1)}, bf16[2,2,64,1024]{3,2,1,0:T(8,128)(2,1)S(1)}, u32[]{:S(2)}, u32[]{:S(2)}) collective-permute-start(bf16[2,2,64,1024]{3,2,1,0:T(8,128)(2,1)S(1)} %get-tuple-element.9.rest_0_), channel_id=1, source_target_pairs={{0,24},{4,28},{8,16},{12,20},{16,8},{20,12},{24,0},{28,4},{1,25},{... | collective-permute-start | bytes 1572872 | tf_op jit(solution)/shard_map/ppermute | solution.py:111
  10.4 0.5 collective-permute-start.1
  10.9 6.3 %collective-permute-done.7 = bf16[1,1,2,2,64,1024]{5,4,3,2,1,0:T(8,128)(2,1)S(1)} collective-permute-done((bf16[1,1,2,2,64,1024]{5,4,3,2,1,0:T(8,128)(2,1)S(1)}, bf16[1,1,2,2,64,1024]{5,4,3,2,1,0:T(8,128)(2,1)S(1)}, u32[]{:S(2)}, u32[]{:S(2)}) %collective-permute-start.7) | collective-permute-done | bytes 524320 | tf_op jit(solution)/shard_map/ppermute | solution.py:141
  17.2 4.1 %collective-permute-done.9 = bf16[1,1,2,2,64,1024]{5,4,3,2,1,0:T(8,128)(2,1)S(1)} collective-permute-done((bf16[1,1,2,2,64,1024]{5,4,3,2,1,0:T(8,128)(2,1)S(1)}, bf16[1,1,2,2,64,1024]{5,4,3,2,1,0:T(8,128)(2,1)S(1)}, u32[]{:S(2)}, u32[]{:S(2)}) %collective-permute-start.9) | collective-permute-done | bytes 524320 | tf_op jit(solution)/shard_map/ppermute | solution.py:141
  21.3 1.5 %collective-permute-start.11 = (bf16[2,2,64,1024]{3,2,1,0:T(8,128)(2,1)S(1)}, bf16[2,2,64,1024]{3,2,1,0:T(8,128)(2,1)}, u32[]{:S(2)}, u32[]{:S(2)}) collective-permute-start(bf16[2,2,64,1024]{3,2,1,0:T(8,128)(2,1)S(1)} %bitcast.36), channel_id=1, source_target_pairs={{0,8},{4,12},{8,0},{12,4},{16,24},{20,28},{24,16},{28,20},{1,9},{5... | collective-permute-start | bytes 1572872 | tf_op jit(solution)/shard_map/ppermute | solution.py:111
  23.2 9.7 %collective-permute-done.3.rest_4_ = bf16[2,2,64,1024]{3,2,1,0:T(8,128)(2,1)S(1)} collective-permute-done((bf16[2,2,64,1024]{3,2,1,0:T(8,128)(2,1)S(1)}, bf16[2,2,64,1024]{3,2,1,0:T(8,128)(2,1)S(1)}, u32[]{:S(2)}, u32[]{:S(2)}) %collective-permute-start.3) | collective-permute-done | bytes 524320 | tf_op jit(solution)/shard_map/ppermute | solution.py:111
  33.0 1.5 %collective-permute-start.17 = (bf16[2,2,64,1024]{3,2,1,0:T(8,128)(2,1)S(1)}, bf16[2,2,64,1024]{3,2,1,0:T(8,128)(2,1)S(1)}, u32[]{:S(2)}, u32[]{:S(2)}) collective-permute-start(bf16[2,2,64,1024]{3,2,1,0:T(8,128)(2,1)S(1)} %bitcast.39), channel_id=1, source_target_pairs={{0,16},{4,20},{8,24},{12,28},{16,0},{20,4},{24,8},{28,12},{1,17},{... | collective-permute-start | bytes 1572872 | tf_op jit(solution)/shard_map/ppermute | solution.py:111
  34.5 0.8 copy-done
  35.4 1.3 %collective-permute-start.21 = (bf16[2,2,64,1024]{3,2,1,0:T(8,128)(2,1)S(1)}, bf16[2,2,64,1024]{3,2,1,0:T(8,128)(2,1)S(1)}, u32[]{:S(2)}, u32[]{:S(2)}) collective-permute-start(bf16[2,2,64,1024]{3,2,1,0:T(8,128)(2,1)S(1)} %collective-permute-done.5.rest_6_), channel_id=1, source_target_pairs={{1,0},{2,1},{3,2},{5,4},{6,5},{7,6},{9,8},{10,9},{11,10},{13,12},{... | collective-permute-start | bytes 1572872 | tf_op jit(solution)/shard_map/ppermute | solution.py:154
  36.7 7.7 %collective-permute-done.11.rest_12_ = bf16[2,2,64,1024]{3,2,1,0:T(8,128)(2,1)} collective-permute-done((bf16[2,2,64,1024]{3,2,1,0:T(8,128)(2,1)S(1)}, bf16[2,2,64,1024]{3,2,1,0:T(8,128)(2,1)}, u32[]{:S(2)}, u32[]{:S(2)}) %collective-permute-start.11) | collective-permute-done | bytes 524320 | tf_op jit(solution)/shard_map/ppermute | solution.py:111
  44.4 4.3 %collective-permute-start.19 = (bf16[2,2,64,1024]{3,2,1,0:T(8,128)(2,1)S(1)}, bf16[2,2,64,1024]{3,2,1,0:T(8,128)(2,1)S(1)}, u32[]{:S(2)}, u32[]{:S(2)}) collective-permute-start(bf16[2,2,64,1024]{3,2,1,0:T(8,128)(2,1)S(1)} %collective-permute-done.5.rest_6_), channel_id=1, source_target_pairs={{0,1},{1,2},{2,3},{4,5},{5,6},{6,7},{8,9},{9,10},{10,11},{12,13},{... | collective-permute-start | bytes 1572872 | tf_op jit(solution)/shard_map/ppermute | solution.py:154
  48.7 0.8 copy-done.2
  49.5 4.2 %collective-permute-start.15 = (bf16[2,2,64,1024]{3,2,1,0:T(8,128)(2,1)S(1)}, bf16[2,2,64,1024]{3,2,1,0:T(8,128)(2,1)}, u32[]{:S(2)}, u32[]{:S(2)}) collective-permute-start(bf16[2,2,64,1024]{3,2,1,0:T(8,128)(2,1)S(1)} %collective-permute-done.3.rest_4_), channel_id=1, source_target_pairs={{0,1},{1,2},{2,3},{4,5},{5,6},{6,7},{8,9},{9,10},{10,11},{12,13},{... | collective-permute-start | bytes 1572872 | tf_op jit(solution)/shard_map/ppermute | solution.py:154
  54.0 1.3 %collective-permute-start.13 = (bf16[2,2,64,1024]{3,2,1,0:T(8,128)(2,1)S(1)}, bf16[2,2,64,1024]{3,2,1,0:T(8,128)(2,1)}, u32[]{:S(2)}, u32[]{:S(2)}) collective-permute-start(bf16[2,2,64,1024]{3,2,1,0:T(8,128)(2,1)S(1)} %collective-permute-done.1.rest_2_), channel_id=1, source_target_pairs={{1,0},{2,1},{3,2},{5,4},{6,5},{7,6},{9,8},{10,9},{11,10},{13,12},{... | collective-permute-start | bytes 1572872 | tf_op jit(solution)/shard_map/ppermute | solution.py:154
  55.3 5.7 %collective-permute-done.19.rest_20_ = bf16[2,2,64,1024]{3,2,1,0:T(8,128)(2,1)S(1)} collective-permute-done((bf16[2,2,64,1024]{3,2,1,0:T(8,128)(2,1)S(1)}, bf16[2,2,64,1024]{3,2,1,0:T(8,128)(2,1)S(1)}, u32[]{:S(2)}, u32[]{:S(2)}) %collective-permute-start.19) | collective-permute-done | bytes 524320 | tf_op jit(solution)/shard_map/ppermute | solution.py:154
  61.0 0.8 copy-done.4
  62.3 0.7 copy-done.12
  63.1 0.6 copy-done.7
  63.7 0.7 gather_fusion
  64.5 0.7 gather_fusion.1
  65.3 4.2 %collective-permute-done.15.rest_16_ = bf16[2,2,64,1024]{3,2,1,0:T(8,128)(2,1)} collective-permute-done((bf16[2,2,64,1024]{3,2,1,0:T(8,128)(2,1)S(1)}, bf16[2,2,64,1024]{3,2,1,0:T(8,128)(2,1)}, u32[]{:S(2)}, u32[]{:S(2)}) %collective-permute-start.15) | collective-permute-done | bytes 524320 | tf_op jit(solution)/shard_map/ppermute | solution.py:154
  71.8 0.7 collective-permute-done.22.rest_23_
  72.6 0.7 collective-permute-done.20.rest_21_
  73.3 0.7 collective-permute-done.16.rest_17_
  74.1 0.7 collective-permute-done.14.rest_15_
  74.8 1.0 %copy-done.1 = bf16[2,2,64,1024]{3,2,1,0:T(8,128)(2,1)S(1)} copy-done((bf16[2,2,64,1024]{3,2,1,0:T(8,128)(2,1)S(1)}, bf16[2,2,64,1024]{3,2,1,0:T(8,128)(2,1)}, u32[]{:S(2)}) %copy-start.1) | copy-done | bytes 524312
  75.9 1.0 %copy-done.3 = bf16[2,2,64,1024]{3,2,1,0:T(8,128)(2,1)S(1)} copy-done((bf16[2,2,64,1024]{3,2,1,0:T(8,128)(2,1)S(1)}, bf16[2,2,64,1024]{3,2,1,0:T(8,128)(2,1)}, u32[]{:S(2)}) %copy-start.3) | copy-done | bytes 524312
  76.9 1.0 %copy-done.5 = bf16[2,2,64,1024]{3,2,1,0:T(8,128)(2,1)S(1)} copy-done((bf16[2,2,64,1024]{3,2,1,0:T(8,128)(2,1)S(1)}, bf16[2,2,64,1024]{3,2,1,0:T(8,128)(2,1)}, u32[]{:S(2)}) %copy-start.5) | copy-done | bytes 524312
  78.0 13.0 %shard_map.73 = bf16[128,1024]{1,0:T(8,128)(2,1)} custom-call(s32[128]{0:T(128)S(1)} %reshape.270.where_ref, s32[2]{0:T(128)S(1)} %clamp_bitcast_fusion.counts_ref, bf16[128,1024]{1,0:T(8,128)(2,1)S(1)} %bitcast.42, bf16[2,2,64,1024]{3,2,1,0:T(8,128)(2,1)S(1)} %get-tuple-element.9.rest_0_, bf16[2,2,64,1024]{3,2,1,0:T(8,128)(2,1)S(1)} %copy-done.1, ...), custom_call_target="tpu_custom_call" | custom-call | tf_op jit(solution)/shard_map/pallas_call | solution.py:101
  (56 shorter events, 4.2 us)
Async XLA Ops:
  1.1 16.1 %collective-permute-start.7 = (bf16[1,1,2,2,64,1024]{5,4,3,2,1,0:T(8,128)(2,1)S(1)}, bf16[1,1,2,2,64,1024]{5,4,3,2,1,0:T(8,128)(2,1)S(1)}, u32[]{:S(2)}, u32[]{:S(2)}) collective-permute-start(bf16[1,1,2,2,64,1024]{5,4,3,2,1,0:T(8,128)(2,1)S(1)} %get-tuple-element.8), channel_id=1, source_target_pairs={{0,1},{1,2},{2,3},{4,5},{5,6},{6,7},{8,9},{9,10},{10,11},{12,13},{... | collective-permute-start | bytes 1572872 | tf_op jit(solution)/shard_map/ppermute | solution.py:141
  6.1 15.3 %collective-permute-start.9 = (bf16[1,1,2,2,64,1024]{5,4,3,2,1,0:T(8,128)(2,1)S(1)}, bf16[1,1,2,2,64,1024]{5,4,3,2,1,0:T(8,128)(2,1)S(1)}, u32[]{:S(2)}, u32[]{:S(2)}) collective-permute-start(bf16[1,1,2,2,64,1024]{5,4,3,2,1,0:T(8,128)(2,1)S(1)} %get-tuple-element.8), channel_id=1, source_target_pairs={{1,0},{2,1},{3,2},{5,4},{6,5},{7,6},{9,8},{10,9},{11,10},{13,12},{... | collective-permute-start | bytes 1572872 | tf_op jit(solution)/shard_map/ppermute | solution.py:141
  7.4 15.9 %collective-permute-start.5 = (bf16[2,2,64,1024]{3,2,1,0:T(8,128)(2,1)S(1)}, bf16[2,2,64,1024]{3,2,1,0:T(8,128)(2,1)S(1)}, u32[]{:S(2)}, u32[]{:S(2)}) collective-permute-start(bf16[2,2,64,1024]{3,2,1,0:T(8,128)(2,1)S(1)} %get-tuple-element.9.rest_0_), channel_id=1, source_target_pairs={{0,24},{4,28},{8,16},{12,20},{16,8},{20,12},{24,0},{28,4},{1,25},{... | collective-permute-start | bytes 1572872 | tf_op jit(solution)/shard_map/ppermute | solution.py:111
  9.9 23.1 %collective-permute-start.3 = (bf16[2,2,64,1024]{3,2,1,0:T(8,128)(2,1)S(1)}, bf16[2,2,64,1024]{3,2,1,0:T(8,128)(2,1)S(1)}, u32[]{:S(2)}, u32[]{:S(2)}) collective-permute-start(bf16[2,2,64,1024]{3,2,1,0:T(8,128)(2,1)S(1)} %get-tuple-element.9.rest_0_), channel_id=1, source_target_pairs={{0,16},{4,20},{8,24},{12,28},{16,0},{20,4},{24,8},{28,12},{1,17},{... | collective-permute-start | bytes 1572872 | tf_op jit(solution)/shard_map/ppermute | solution.py:111
  10.4 24.1 %collective-permute-start.1 = (bf16[2,2,64,1024]{3,2,1,0:T(8,128)(2,1)S(1)}, bf16[2,2,64,1024]{3,2,1,0:T(8,128)(2,1)S(1)}, u32[]{:S(2)}, u32[]{:S(2)}) collective-permute-start(bf16[2,2,64,1024]{3,2,1,0:T(8,128)(2,1)S(1)} %get-tuple-element.9.rest_0_), channel_id=1, source_target_pairs={{0,8},{4,12},{8,0},{12,4},{16,24},{20,28},{24,16},{28,20},{1,9},{5... | collective-permute-start | bytes 1572872 | tf_op jit(solution)/shard_map/ppermute | solution.py:111
  17.2 17.3 %collective-permute-start = (bf16[2,2,64,1024]{3,2,1,0:T(8,128)(2,1)S(1)}, bf16[2,2,64,1024]{3,2,1,0:T(8,128)(2,1)S(1)}, u32[]{:S(2)}, u32[]{:S(2)}) collective-permute-start(bf16[2,2,64,1024]{3,2,1,0:T(8,128)(2,1)S(1)} %get-tuple-element.9.rest_0_), channel_id=1, source_target_pairs={{0,4},{4,0},{8,12},{12,8},{16,20},{20,16},{24,28},{28,24},{1,5},{5... | collective-permute-start | bytes 1572872 | tf_op jit(solution)/shard_map/ppermute | solution.py:111
  21.3 23.0 %collective-permute-start.11 = (bf16[2,2,64,1024]{3,2,1,0:T(8,128)(2,1)S(1)}, bf16[2,2,64,1024]{3,2,1,0:T(8,128)(2,1)}, u32[]{:S(2)}, u32[]{:S(2)}) collective-permute-start(bf16[2,2,64,1024]{3,2,1,0:T(8,128)(2,1)S(1)} %bitcast.36), channel_id=1, source_target_pairs={{0,8},{4,12},{8,0},{12,4},{16,24},{20,28},{24,16},{28,20},{1,9},{5... | collective-permute-start | bytes 1572872 | tf_op jit(solution)/shard_map/ppermute | solution.py:111
  23.2 25.5 %collective-permute-start.8 = (bf16[2,2,64,1024]{3,2,1,0:T(8,128)(2,1)S(1)}, bf16[2,2,64,1024]{3,2,1,0:T(8,128)(2,1)S(1)}, u32[]{:S(2)}, u32[]{:S(2)}) collective-permute-start(bf16[2,2,64,1024]{3,2,1,0:T(8,128)(2,1)S(1)} %bitcast.37), channel_id=1, source_target_pairs={{0,4},{4,0},{8,12},{12,8},{16,20},{20,16},{24,28},{28,24},{1,5},{5... | collective-permute-start | bytes 1572872 | tf_op jit(solution)/shard_map/ppermute | solution.py:111
  33.0 16.6 %collective-permute-start.17 = (bf16[2,2,64,1024]{3,2,1,0:T(8,128)(2,1)S(1)}, bf16[2,2,64,1024]{3,2,1,0:T(8,128)(2,1)S(1)}, u32[]{:S(2)}, u32[]{:S(2)}) collective-permute-start(bf16[2,2,64,1024]{3,2,1,0:T(8,128)(2,1)S(1)} %bitcast.39), channel_id=1, source_target_pairs={{0,16},{4,20},{8,24},{12,28},{16,0},{20,4},{24,8},{28,12},{1,17},{... | collective-permute-start | bytes 1572872 | tf_op jit(solution)/shard_map/ppermute | solution.py:111
  34.5 19.2 %collective-permute-start.10 = (bf16[2,2,64,1024]{3,2,1,0:T(8,128)(2,1)S(1)}, bf16[2,2,64,1024]{3,2,1,0:T(8,128)(2,1)S(1)}, u32[]{:S(2)}, u32[]{:S(2)}) collective-permute-start(bf16[2,2,64,1024]{3,2,1,0:T(8,128)(2,1)S(1)} %bitcast.40), channel_id=1, source_target_pairs={{0,4},{4,0},{8,12},{12,8},{16,20},{20,16},{24,28},{28,24},{1,5},{5... | collective-permute-start | bytes 1572872 | tf_op jit(solution)/shard_map/ppermute | solution.py:111
  34.5 0.8 copy-start
  35.4 18.6 %collective-permute-start.21 = (bf16[2,2,64,1024]{3,2,1,0:T(8,128)(2,1)S(1)}, bf16[2,2,64,1024]{3,2,1,0:T(8,128)(2,1)S(1)}, u32[]{:S(2)}, u32[]{:S(2)}) collective-permute-start(bf16[2,2,64,1024]{3,2,1,0:T(8,128)(2,1)S(1)} %collective-permute-done.5.rest_6_), channel_id=1, source_target_pairs={{1,0},{2,1},{3,2},{5,4},{6,5},{7,6},{9,8},{10,9},{11,10},{13,12},{... | collective-permute-start | bytes 1572872 | tf_op jit(solution)/shard_map/ppermute | solution.py:154
  44.4 16.6 %collective-permute-start.19 = (bf16[2,2,64,1024]{3,2,1,0:T(8,128)(2,1)S(1)}, bf16[2,2,64,1024]{3,2,1,0:T(8,128)(2,1)S(1)}, u32[]{:S(2)}, u32[]{:S(2)}) collective-permute-start(bf16[2,2,64,1024]{3,2,1,0:T(8,128)(2,1)S(1)} %collective-permute-done.5.rest_6_), channel_id=1, source_target_pairs={{0,1},{1,2},{2,3},{4,5},{5,6},{6,7},{8,9},{9,10},{10,11},{12,13},{... | collective-permute-start | bytes 1572872 | tf_op jit(solution)/shard_map/ppermute | solution.py:154
  49.5 11.5 %collective-permute-start.6 = (bf16[2,2,64,1024]{3,2,1,0:T(8,128)(2,1)S(1)}, bf16[2,2,64,1024]{3,2,1,0:T(8,128)(2,1)S(1)}, u32[]{:S(2)}, u32[]{:S(2)}) collective-permute-start(bf16[2,2,64,1024]{3,2,1,0:T(8,128)(2,1)S(1)} %collective-permute-done.5.rest_6_), channel_id=1, source_target_pairs={{0,4},{4,0},{8,12},{12,8},{16,20},{20,16},{24,28},{28,24},{1,5},{5... | collective-permute-start | bytes 1572872 | tf_op jit(solution)/shard_map/ppermute | solution.py:111
  49.5 11.5 %copy-start.8 = (bf16[2,2,64,1024]{3,2,1,0:T(8,128)(2,1)}, bf16[2,2,64,1024]{3,2,1,0:T(8,128)(2,1)S(1)}, u32[]{:S(2)}) copy-start(bf16[2,2,64,1024]{3,2,1,0:T(8,128)(2,1)S(1)} %collective-permute-done.17.rest_18_) | copy-start | bytes 1572868
  49.5 20.0 %collective-permute-start.15 = (bf16[2,2,64,1024]{3,2,1,0:T(8,128)(2,1)S(1)}, bf16[2,2,64,1024]{3,2,1,0:T(8,128)(2,1)}, u32[]{:S(2)}, u32[]{:S(2)}) collective-permute-start(bf16[2,2,64,1024]{3,2,1,0:T(8,128)(2,1)S(1)} %collective-permute-done.3.rest_4_), channel_id=1, source_target_pairs={{0,1},{1,2},{2,3},{4,5},{5,6},{6,7},{8,9},{9,10},{10,11},{12,13},{... | collective-permute-start | bytes 1572872 | tf_op jit(solution)/shard_map/ppermute | solution.py:154
  53.8 8.6 %copy-start.9 = (bf16[2,2,64,1024]{3,2,1,0:T(8,128)(2,1)}, bf16[2,2,64,1024]{3,2,1,0:T(8,128)(2,1)S(1)}, u32[]{:S(2)}) copy-start(bf16[2,2,64,1024]{3,2,1,0:T(8,128)(2,1)S(1)} %collective-permute-done.10.rest_11_) | copy-start | bytes 1572868
  53.8 15.8 %collective-permute-start.4 = (bf16[2,2,64,1024]{3,2,1,0:T(8,128)(2,1)S(1)}, bf16[2,2,64,1024]{3,2,1,0:T(8,128)(2,1)}, u32[]{:S(2)}, u32[]{:S(2)}) collective-permute-start(bf16[2,2,64,1024]{3,2,1,0:T(8,128)(2,1)S(1)} %collective-permute-done.3.rest_4_), channel_id=1, source_target_pairs={{0,4},{4,0},{8,12},{12,8},{16,20},{20,16},{24,28},{28,24},{1,5},{5... | collective-permute-start | bytes 1572872 | tf_op jit(solution)/shard_map/ppermute | solution.py:111
  54.0 8.3 %copy-start.10 = (bf16[2,2,64,1024]{3,2,1,0:T(8,128)(2,1)}, bf16[2,2,64,1024]{3,2,1,0:T(8,128)(2,1)S(1)}, u32[]{:S(2)}) copy-start(bf16[2,2,64,1024]{3,2,1,0:T(8,128)(2,1)S(1)} %collective-permute-done.21.rest_22_) | copy-start | bytes 1572868
  54.0 16.1 %collective-permute-start.13 = (bf16[2,2,64,1024]{3,2,1,0:T(8,128)(2,1)S(1)}, bf16[2,2,64,1024]{3,2,1,0:T(8,128)(2,1)}, u32[]{:S(2)}, u32[]{:S(2)}) collective-permute-start(bf16[2,2,64,1024]{3,2,1,0:T(8,128)(2,1)S(1)} %collective-permute-done.1.rest_2_), channel_id=1, source_target_pairs={{1,0},{2,1},{3,2},{5,4},{6,5},{7,6},{9,8},{10,9},{11,10},{13,12},{... | collective-permute-start | bytes 1572872 | tf_op jit(solution)/shard_map/ppermute | solution.py:154
  61.0 1.3 %copy-start.11 = (bf16[2,2,64,1024]{3,2,1,0:T(8,128)(2,1)}, bf16[2,2,64,1024]{3,2,1,0:T(8,128)(2,1)S(1)}, u32[]{:S(2)}) copy-start(bf16[2,2,64,1024]{3,2,1,0:T(8,128)(2,1)S(1)} %collective-permute-done.19.rest_20_) | copy-start | bytes 1572868
  61.0 9.1 %collective-permute-start.2 = (bf16[2,2,64,1024]{3,2,1,0:T(8,128)(2,1)S(1)}, bf16[2,2,64,1024]{3,2,1,0:T(8,128)(2,1)}, u32[]{:S(2)}, u32[]{:S(2)}) collective-permute-start(bf16[2,2,64,1024]{3,2,1,0:T(8,128)(2,1)S(1)} %collective-permute-done.1.rest_2_), channel_id=1, source_target_pairs={{0,4},{4,0},{8,12},{12,8},{16,20},{20,16},{24,28},{28,24},{1,5},{5... | collective-permute-start | bytes 1572872 | tf_op jit(solution)/shard_map/ppermute | solution.py:111
  61.8 8.8 %collective-permute-start.12 = (bf16[2,2,64,1024]{3,2,1,0:T(8,128)(2,1)}, bf16[2,2,64,1024]{3,2,1,0:T(8,128)(2,1)}, u32[]{:S(2)}, u32[]{:S(2)}) collective-permute-start(bf16[2,2,64,1024]{3,2,1,0:T(8,128)(2,1)} %collective-permute-done.11.rest_12_), channel_id=1, source_target_pairs={{0,4},{4,0},{8,12},{12,8},{16,20},{20,16},{24,28},{28,24},{1,5},{5... | collective-permute-start | bytes 1572872 | tf_op jit(solution)/shard_map/ppermute | solution.py:111
  64.5 10.3 %copy-start.6 = (bf16[1,1,128,1024]{3,2,1,0:T(8,128)(2,1)S(1)}, bf16[1,1,128,1024]{3,2,1,0:T(8,128)(2,1)}, u32[]{:S(2)}) copy-start(bf16[1,1,128,1024]{3,2,1,0:T(8,128)(2,1)} %param.7) | copy-start | bytes 786436
  69.6 2.3 %collective-permute-start.18 = (bf16[2,2,64,1024]{3,2,1,0:T(8,128)(2,1)}, bf16[2,2,64,1024]{3,2,1,0:T(8,128)(2,1)}, u32[]{:S(2)}, u32[]{:S(2)}) collective-permute-start(bf16[2,2,64,1024]{3,2,1,0:T(8,128)(2,1)} %copy-done.8), channel_id=1, source_target_pairs={{0,4},{4,0},{8,12},{12,8},{16,20},{20,16},{24,28},{28,24},{1,5},{5... | collective-permute-start | bytes 1572872 | tf_op jit(solution)/shard_map/ppermute | solution.py:111
  69.6 3.0 %collective-permute-start.22 = (bf16[2,2,64,1024]{3,2,1,0:T(8,128)(2,1)}, bf16[2,2,64,1024]{3,2,1,0:T(8,128)(2,1)}, u32[]{:S(2)}, u32[]{:S(2)}) collective-permute-start(bf16[2,2,64,1024]{3,2,1,0:T(8,128)(2,1)} %copy-done.10), channel_id=1, source_target_pairs={{0,4},{4,0},{8,12},{12,8},{16,20},{20,16},{24,28},{28,24},{1,5},{5... | collective-permute-start | bytes 1572872 | tf_op jit(solution)/shard_map/ppermute | solution.py:111
  70.1 3.2 %collective-permute-start.20 = (bf16[2,2,64,1024]{3,2,1,0:T(8,128)(2,1)}, bf16[2,2,64,1024]{3,2,1,0:T(8,128)(2,1)}, u32[]{:S(2)}, u32[]{:S(2)}) collective-permute-start(bf16[2,2,64,1024]{3,2,1,0:T(8,128)(2,1)} %copy-done.11), channel_id=1, source_target_pairs={{0,4},{4,0},{8,12},{12,8},{16,20},{20,16},{24,28},{28,24},{1,5},{5... | collective-permute-start | bytes 1572872 | tf_op jit(solution)/shard_map/ppermute | solution.py:111
  70.2 3.9 %collective-permute-start.16 = (bf16[2,2,64,1024]{3,2,1,0:T(8,128)(2,1)}, bf16[2,2,64,1024]{3,2,1,0:T(8,128)(2,1)}, u32[]{:S(2)}, u32[]{:S(2)}) collective-permute-start(bf16[2,2,64,1024]{3,2,1,0:T(8,128)(2,1)} %collective-permute-done.15.rest_16_), channel_id=1, source_target_pairs={{0,4},{4,0},{8,12},{12,8},{16,20},{20,16},{24,28},{28,24},{1,5},{5... | collective-permute-start | bytes 1572872 | tf_op jit(solution)/shard_map/ppermute | solution.py:111
  70.6 4.2 %collective-permute-start.14 = (bf16[2,2,64,1024]{3,2,1,0:T(8,128)(2,1)}, bf16[2,2,64,1024]{3,2,1,0:T(8,128)(2,1)}, u32[]{:S(2)}, u32[]{:S(2)}) collective-permute-start(bf16[2,2,64,1024]{3,2,1,0:T(8,128)(2,1)} %collective-permute-done.13.rest_14_), channel_id=1, source_target_pairs={{0,4},{4,0},{8,12},{12,8},{16,20},{20,16},{24,28},{28,24},{1,5},{5... | collective-permute-start | bytes 1572872 | tf_op jit(solution)/shard_map/ppermute | solution.py:111
  74.8 1.0 %copy-start.1 = (bf16[2,2,64,1024]{3,2,1,0:T(8,128)(2,1)S(1)}, bf16[2,2,64,1024]{3,2,1,0:T(8,128)(2,1)}, u32[]{:S(2)}) copy-start(bf16[2,2,64,1024]{3,2,1,0:T(8,128)(2,1)} %copy-done) | copy-start | bytes 1572868
  75.9 1.0 %copy-start.3 = (bf16[2,2,64,1024]{3,2,1,0:T(8,128)(2,1)S(1)}, bf16[2,2,64,1024]{3,2,1,0:T(8,128)(2,1)}, u32[]{:S(2)}) copy-start(bf16[2,2,64,1024]{3,2,1,0:T(8,128)(2,1)} %copy-done.2) | copy-start | bytes 1572868
  76.9 1.0 %copy-start.5 = (bf16[2,2,64,1024]{3,2,1,0:T(8,128)(2,1)S(1)}, bf16[2,2,64,1024]{3,2,1,0:T(8,128)(2,1)}, u32[]{:S(2)}) copy-start(bf16[2,2,64,1024]{3,2,1,0:T(8,128)(2,1)} %copy-done.4) | copy-start | bytes 1572868
  (5 other events, 3.7 us)
